TPU v7x, 32 devices: a whole 2x2x4 slice. The times are simulated.
32 devices in a mesh: tile: 4 (over y, core), orient: 8 (over z, x).
Axes of the slice: x: 2, y: 2, z: 4, core: 2. Of those that a mesh axis runs over, the one named last changes fastest.
Arguments:
- tile_spectra: bfloat16 [4, 2, 512, 512], P('tile', None, 'orient'), may hold values from -6 to 6
- template_spectra: bfloat16 [64, 2, 512, 512], P('orient', None, 'tile'), may hold values from -6 to 6
- peaks: int32 [4, 4, 2], P('tile'), may hold values from 0 to 511
- listed: int32 [4, 4, 48], P('tile'), may hold values from 0 to 63, as said below
Outputs:
- best: float32 [4, 4, 128, 128], P('tile')
- power: float32 [4, 4, 128, 128], P('tile')
Inputs may be any that keep to these rules, and one draw needn't show every extreme that they name: The 48 ids listed for one peak are distinct.
All inputs are finite; a program needn't handle non-finite values.
Results may differ from a plain program's by a relative error of at most 0.0026.
Values may be sent and summed in bfloat16 or wider, within the bound.
No kernel may reach another device: no remote copies, remote signals or barrier semaphores. Data moves between devices by JAX's collectives and lax.ppermute only.
A program may use at most 128 MiB of HBM per device.

v0:
```python
import math
import jax
import jax.numpy as jnp
from jax import lax
from jax.sharding import PartitionSpec as P

W = 128
LIST = 48
lowest_score = -1e30


def combined_all(shard, axis, combine):
    everything = jax.tree.map(lambda part: lax.all_gather(part, axis), shard)
    first = jax.tree.map(lambda part: part[0], everything)

    def lap(k, so_far):
        return combine(so_far, jax.tree.map(lambda part: part[k], everything))

    return lax.fori_loop(1, lax.axis_size(axis), lap, first)


def window_tables(peak_rows, size, width):
    offsets = jnp.arange(width, dtype=jnp.int32) - width // 2
    freqs = jnp.arange(size, dtype=jnp.int32)

    def tables_for(coords):
        position = (coords[:, None] + offsets[None, :]) % size
        phase = freqs[None, :, None] * position[:, None, :] % size
        angle = phase.astype(jnp.float32) * (2.0 * math.pi / size)
        return (jnp.cos(angle).astype(jnp.bfloat16), jnp.sin(angle).astype(jnp.bfloat16))

    cos_row, sin_row = tables_for(peak_rows[:, 0])
    cos_col, sin_col = tables_for(peak_rows[:, 1])
    upper = jnp.concatenate([cos_col, sin_col], axis=-1)
    lower = jnp.concatenate([-sin_col, cos_col], axis=-1)
    return (cos_row, sin_row, jnp.concatenate([upper, lower], axis=1))


def cross_spectrum(spectrum, template):
    image_re = spectrum[0].astype(jnp.float32)
    image_im = spectrum[1].astype(jnp.float32)
    tmpl_re = template[..., 0, :, :].astype(jnp.float32)
    tmpl_im = template[..., 1, :, :].astype(jnp.float32)
    mixed_re = image_re * tmpl_re + image_im * tmpl_im
    mixed_im = image_im * tmpl_re - image_re * tmpl_im
    return jnp.concatenate([mixed_re, mixed_im], axis=-1).astype(jnp.bfloat16)


def joint_reduce(first_pair, second_pair):
    return (jnp.maximum(first_pair[0], second_pair[0]), first_pair[1] + second_pair[1])


def reduce_orient(best_part, power_part):
    return combined_all((best_part, power_part), "orient", joint_reduce)


def local(tile_spectra, template_spectra, peaks, listed):
    size = tile_spectra.shape[3]
    width = W
    cos_row, sin_row, col_table = window_tables(peaks[0], size, width)
    listed_ids = listed[0]
    spectrum = lax.all_gather(tile_spectra, "orient", axis=2, tiled=True)[0]
    block_size = template_spectra.shape[0]
    mixed = cross_spectrum(spectrum, lax.all_gather(template_spectra, "tile", axis=2, tiled=True))
    partial_g = jnp.einsum(
        "jnk,pkw->pjnw", mixed, col_table, preferred_element_type=jnp.float32
    ).astype(jnp.bfloat16)
    update = jnp.einsum(
        "pna,pjnb->pjab", cos_row, partial_g[..., :width], preferred_element_type=jnp.float32
    )
    update = update - jnp.einsum(
        "pna,pjnb->pjab", sin_row, partial_g[..., width:], preferred_element_type=jnp.float32
    )
    scores = update / size
    global_ids = lax.axis_index("orient") * block_size + jnp.arange(block_size, dtype=jnp.int32)
    is_listed = jnp.any(listed_ids[:, :, None] == global_ids[None, None, :], axis=1)
    is_listed = is_listed[:, :, None, None]
    best_part = jnp.max(jnp.where(is_listed, scores, lowest_score), axis=1)
    power_part = jnp.sum(jnp.where(is_listed, scores * scores, 0.0), axis=1)
    best_all, power_all = reduce_orient(best_part, power_part)
    return (best_all[None], (power_all / LIST)[None])


def solution(mesh):
    placed = (
        P("tile", None, "orient", None),
        P("orient", None, "tile", None),
        P("tile", None, None),
        P("tile", None, None),
    )
    return jax.shard_map(
        local,
        mesh=mesh,
        in_specs=placed,
        out_specs=(P("tile", None, None, None), P("tile", None, None, None)),
        check_vma=False,
    )
```

profile of v0, /device:TPU:0, one launch (start us, length us, event | category | flops | bytes accessed | tf_op | source)
XLA Modules:
  0.0 261.0 jit_solution(14473625510305335943)
XLA Ops:
  7.2 0.0 all-gather.7.cloned.1.call-start
  7.2 0.7 all-gather.7.cloned.1.call-update
  7.9 0.0 all-gather.9.cloned.1.call-start
  8.0 3.1 %copy.14 = bf16[8,2,128,512]{3,2,0,1:T(8,128)(2,1)} copy(bf16[8,2,128,512]{3,2,1,0:T(8,128)(2,1)} %param.7) | data formatting | bytes 4194304 | tf_op args[1]
  11.1 0.0 all-gather.11.cloned.1.call-start
  11.2 0.2 compare_reduce_fusion
  11.5 0.1 add_select_fusion.4
  11.5 4.3 %fusion.39 = bf16[4,512,128]{1,2,0:T(8,128)(2,1)S(1)} fusion(s32[4,128]{1,0:T(4,128)S(1)} %get-tuple-element.160), kind=kLoop, calls=%fused_computation.60 | loop fusion | flops 4718592 | bytes 526336 | tf_op jit(solution)/shard_map/neg | solution.py:35
  15.8 5.6 %sine_convert_fusion.1 = (bf16[4,512,128]{1,2,0:T(8,128)(2,1)S(1)}, bf16[4,512,128]{1,2,0:T(8,128)(2,1)}) fusion(s32[4,128]{1,0:T(4,128)S(1)} %get-tuple-element.160), kind=kLoop, calls=%fused_computation.47 | loop fusion | flops 4194304 | bytes 1050624 | tf_op jit(solution)/shard_map/convert_element_type | solution.py:30
  21.4 31.8 %all-gather.7.cloned.1.call-done = bf16[1,2,512,512]{3,2,1,0:T(8,128)(2,1)} async-done(((bf16[1,2,64,512]{3,2,1,0:T(8,128)(2,1)}), bf16[1,2,512,512]{3,2,1,0:T(8,128)(2,1)}) %all-gather.7.cloned.1.call-update) | async-done | bytes 1048592 | tf_op jit(solution)/shard_map/all_gather | solution.py:62
  53.2 1.5 fusion.36
  54.7 57.1 %all-gather.9.cloned.1.call-done = bf16[8,2,512,512]{3,2,0,1:T(8,128)(2,1)} async-done(((bf16[8,2,128,512]{3,2,0,1:T(8,128)(2,1)}), bf16[8,2,512,512]{3,2,0,1:T(8,128)(2,1)}) %all-gather.9.cloned.1.call-update) | async-done | bytes 8388624 | tf_op jit(solution)/shard_map/all_gather | solution.py:64
  111.8 6.1 %fusion.1 = (bf16[8,512,512]{2,1,0:T(8,128)(2,1)S(1)}, bf16[8,512,512]{2,1,0:T(8,128)(2,1)}) fusion(f32[512,512]{1,0:T(8,128)S(1)} %get-tuple-element.154, f32[512,512]{1,0:T(8,128)S(1)} %get-tuple-element.153, bf16[8,2,512,512]{3,2,0,1:T(8,128)(2,1)} %all-gather.9.cloned.1.call-done), kind=kLoop, calls=%fused_computation.7 | loop fusion | flops 20971520 | bytes 18874368 | tf_op jit(solution)/shard_map/convert.4
  117.9 12.7 %convert_bitcast_fusion = bf16[4,8,512,256]{2,3,1,0:T(8,128)(2,1)} fusion(bf16[8,512,512]{2,1,0:T(8,128)(2,1)} %get-tuple-element.152, bf16[8,512,512]{2,1,0:T(8,128)(2,1)S(1)} %get-tuple-element.151, bf16[4,512,128]{1,2,0:T(8,128)(2,1)S(1)} %copy-done.1, bf16[4,512,128]{1,2,0:T(8,128)(2,1)S(1)} %fusion.39, bf16[4,512,128]{1,2,0:T(8,128)(2,1)S(1)} %get-tuple-element.155), kind=kOutput, calls=%fused_computation.14 | convolution fusion | flops 8619294720 | bytes 18350080 | tf_op jit(solution)/shard_map/jnk,pkw->pjnw/dot_general | solution.py:65
  130.7 7.2 %fusion.7 = f32[4,8,128,128]{3,2,1,0:T(8,128)S(1)} fusion(bf16[4,8,512,256]{2,3,1,0:T(8,128)(2,1)} %convert_bitcast_fusion, s32[4,128]{1,0:T(4,128)S(1)} %get-tuple-element.159), kind=kOutput, calls=%fused_computation.15 | convolution fusion | flops 540803072 | bytes 6293504 | tf_op jit(solution)/shard_map/pna,pjnb->pjab/dot_general | solution.py:71
  137.9 5.8 %select_reduce_fusion = (f32[4,128,128]{2,1,0:T(8,128)S(1)}, f32[4,128,128]{2,1,0:T(8,128)S(1)}) fusion(pred[4,8]{1,0:T(4,128)(4,1)S(1)} %compare_reduce_fusion, f32[4,8,128,128]{3,2,1,0:T(8,128)S(1)} %fusion.7, s32[4,128]{1,0:T(4,128)S(1)} %get-tuple-element.159, bf16[4,8,512,256]{2,3,1,0:T(8,128)(2,1)S(1)} %copy-done.4), kind=kOutput, calls=%fused_computation.28 | convolution fusion | flops 544342016 | bytes 6818304 | tf_op jit(solution)/shard_map/pna,pjnb->pjab/dot_general | solution.py:68
  143.7 0.8 copy.17
  144.6 0.0 all-gather.13.cloned.1.call-start
  144.6 0.8 copy.18
  145.5 48.5 %all-gather.11.cloned.1.call-done = f32[32,128,128]{2,1,0:T(8,128)} async-done(((f32[4,128,128]{2,1,0:T(8,128)}), f32[32,128,128]{2,1,0:T(8,128)}) %all-gather.11.cloned.1.call-update) | async-done | bytes 2097168 | tf_op jit(solution)/shard_map/all_gather | solution.py:13
  194.0 1.0 slice.50
  195.0 49.4 %all-gather.13.cloned.1.call-done = f32[32,128,128]{2,1,0:T(8,128)} async-done(((f32[4,128,128]{2,1,0:T(8,128)}), f32[32,128,128]{2,1,0:T(8,128)}) %all-gather.13.cloned.1.call-update) | async-done | bytes 2097168 | tf_op jit(solution)/shard_map/all_gather | solution.py:13
  244.4 1.0 slice.51
  245.3 8.4 %while.17 = (s32[]{:T(128)}, f32[4,128,128]{2,1,0:T(8,128)S(1)}, f32[4,128,128]{2,1,0:T(8,128)S(1)}, f32[8,4,128,128]{3,2,1,0:T(8,128)}, f32[8,4,128,128]{3,2,1,0:T(8,128)}, /*index=5*/s32[]{:T(128)}, s32[]{:T(128)}, s32[]{:T(128)}) while((s32[]{:T(128)}, f32[4,128,128]{2,1,0:T(8,128)S(1)}, f32[4,128,128]{2,1,0:T(8,128)S(1)}, ...), condition=%wide.region_4.5_spmd, body=%wide.region_3.4_spmd.sunk | while | flops 131077 | bytes 1572995 | solution.py:19
  245.4 1.2 bitcast_add_fusion.2
  246.5 1.2 bitcast_add_fusion.2
  247.7 1.2 bitcast_add_fusion.2
  248.9 1.2 bitcast_add_fusion.2
  250.1 1.2 bitcast_add_fusion.2
  251.3 1.2 bitcast_add_fusion.2
  252.5 1.2 bitcast_add_fusion.2
  253.7 0.8 multiply_bitcast_fusion
  (16 shorter events, 0.1 us)
Async XLA Ops:
  7.2 4.1 %copy-start.2 = (s32[1,4,48]{2,1,0:T(4,128)S(1)}, s32[1,4,48]{2,1,0:T(4,128)}, u32[]{:S(2)}) copy-start(s32[1,4,48]{2,1,0:T(4,128)} %param.9) | copy-start | bytes 2308
  7.2 4.3 %copy-start.3 = (s32[1,4,2]{1,2,0:T(2,128)S(1)}, s32[1,4,2]{1,2,0:T(2,128)}, u32[]{:S(2)}) copy-start(s32[1,4,2]{1,2,0:T(2,128)} %param.8) | copy-start | bytes 100
  7.2 46.0 %all-gather.7.cloned.1.call-start = ((), (), s32[]{:S(2)}) async-start(), calls=%async_computation | async-start | bytes 1179648 | tf_op jit(solution)/shard_map/all_gather | solution.py:62
  7.9 103.9 %all-gather.9.cloned.1.call-start = ((), (), s32[]{:S(2)}) async-start(), calls=%async_computation.1 | async-start | bytes 10485760 | tf_op jit(solution)/shard_map/all_gather | solution.py:64
  11.1 182.9 %all-gather.11.cloned.1.call-start = ((), (), s32[]{:S(2)}) async-start(), calls=%async_computation.2 | async-start | bytes 2359296 | tf_op jit(solution)/shard_map/all_gather | solution.py:13
  111.8 6.1 %copy-start.1 = (bf16[4,512,128]{1,2,0:T(8,128)(2,1)S(1)}, bf16[4,512,128]{1,2,0:T(8,128)(2,1)}, u32[]{:S(2)}) copy-start(bf16[4,512,128]{1,2,0:T(8,128)(2,1)} %get-tuple-element.156) | copy-start | bytes 1572868
  130.7 7.2 %copy-start.4 = (bf16[4,8,512,256]{2,3,1,0:T(8,128)(2,1)S(1)}, bf16[4,8,512,256]{2,3,1,0:T(8,128)(2,1)}, u32[]{:S(2)}) copy-start(bf16[4,8,512,256]{2,3,1,0:T(8,128)(2,1)} %convert_bitcast_fusion) | copy-start | bytes 25165828
  144.6 99.8 %all-gather.13.cloned.1.call-start = ((), (), s32[]{:S(2)}) async-start(), calls=%async_computation.3 | async-start | bytes 2359296 | tf_op jit(solution)/shard_map/all_gather | solution.py:13
  253.7 0.8 copy-start
Sparse Core Ops, SparseCore 0:
  10.2 42.9 all-gather.6
  54.7 57.0 all-gather.8
  144.7 49.2 all-gather.10
  196.6 47.7 all-gather.12
where the time goes:
time: 261 us
  waiting for transfers between devices  188 us (72%)
  other arithmetic  26.7 us (10%)
  matrix products  25.7 us (10%)
  between operations  13.9 us (5%)
  local copies, waits for them, and re-layouts  6.78 us (3%)
    all_gather x2, waiting for transfers between devices, combined_all(): everything = jax.tree.map(lambda part: lax.all_gather(part, axis), shard)  97.9 us
    all_gather x1, waiting for transfers between devices, local(): lax.all_gather(template_spectra, 'tile', axis=2, tiled=True)  57.1 us
    all_gather x1, waiting for transfers between devices, local(): spectrum = lax.all_gather(tile_spectra, 'orient', axis=2, tiled=True)[0]  31.8 us
    dot_general x1, matrix products, local(): jnp.einsum('jnk,pkw->pjnw', mixed, col_table, preferred_element_type=jnp....  12.7 us
    add x7, other arithmetic, joint_reduce(): first_pair[1] + second_pair[1]  8.2 us
    dot_general x1, matrix products, local(): jnp.einsum('pna,pjnb->pjab', sin_row, partial_g[..., width:], preferred_e...  7.18 us
    another operation x1, other arithmetic  6.12 us
    dot_general x1, matrix products, local(): jnp.einsum('pna,pjnb->pjab', cos_row, partial_g[..., :width], preferred_e...  5.83 us
  transfers between devices with their start and end apart: 4, of which 4 were waited for; matrix products, arithmetic and copies ran while one was open for 6% of the time, Pallas kernels for 0%

commit v1 on v0

--- a/solution.py
+++ b/solution.py
@@ -1,3 +1,4 @@
+import functools
 import math
 import jax
 import jax.numpy as jnp
@@ -7,6 +8,26 @@
 W = 128
 LIST = 48
 lowest_score = -1e30
+
+
+def _plan_gates(message, d0):
+    y = list(message.shape[1:])
+    y[d0] *= message.shape[0]
+    return jnp.moveaxis(message, 0, d0).reshape(y)
+
+
+def draft_the_sample(raw, axis_id, k_dim):
+    chips = lax.axis_size(axis_id)
+    by_rank = list(map(lambda no: (no, (no + 1) % chips), range(chips)))
+    leaves = [raw]
+    while len(leaves) < chips:
+        leaves.append(lax.ppermute(leaves[-1], axis_id, perm=by_rank))
+    work_now = lax.axis_index(axis_id)
+    leaves = jnp.stack(leaves)[(work_now - jnp.arange(chips)) % chips]
+    return _plan_gates(leaves, k_dim)
+
+
+ports_meet = functools.partial(draft_the_sample, axis_id="orient", k_dim=2)
 
 
 def combined_all(shard, axis, combine):
@@ -59,7 +80,7 @@
     width = W
     cos_row, sin_row, col_table = window_tables(peaks[0], size, width)
     listed_ids = listed[0]
-    spectrum = lax.all_gather(tile_spectra, "orient", axis=2, tiled=True)[0]
+    spectrum = ports_meet(tile_spectra)[0]
     block_size = template_spectra.shape[0]
     mixed = cross_spectrum(spectrum, lax.all_gather(template_spectra, "tile", axis=2, tiled=True))
     partial_g = jnp.einsum(

time: 261 us -> 222 us (0.85)
  waiting for transfers between devices: 188 us -> 143 us
  starting transfers between devices: 0.16 us -> 4.73 us
    all_gather x1, waiting for transfers between devices: 57.1 us -> 0.02 us  [local(): lax.all_gather(template_spectra, 'tile', axis=2, tiled=True)]
    ppermute x0 -> x7, waiting for transfers between devices: none -> 45.3 us  [draft_the_sample(): leaves.append(lax.ppermute(leaves[-1], axis_id, perm=by_rank))]
    all_gather x1 -> x0, waiting for transfers between devices: 31.8 us -> none  [local(): spectrum = lax.all_gather(tile_spectra, 'orient', axis=2, tiled=True)[0]]
    ppermute x0 -> x7, starting transfers between devices: none -> 4.6 us  [draft_the_sample(): leaves.append(lax.ppermute(leaves[-1], axis_id, perm=by_rank))]
  transfers between devices with their start and end apart: 4 -> 10, of which waited for: 4 -> 8; matrix products, arithmetic and copies ran while one was open for 6% -> 6% of each run, Pallas kernels for 0% -> 0%
where the time goes in v1:
time: 222 us; the launch traced here: 221 us
  waiting for transfers between devices  143 us (64%)
  matrix products  25.8 us (12%)
  other arithmetic  25.7 us (12%)
  between operations  14 us (6%)
  local copies, waits for them, and re-layouts  7.61 us (3%)
  starting transfers between devices  4.73 us (2%)
    all_gather x2, waiting for transfers between devices, combined_all(): everything = jax.tree.map(lambda part: lax.all_gather(part, axis), shard)  97.8 us
    ppermute x7, waiting for transfers between devices, draft_the_sample(): leaves.append(lax.ppermute(leaves[-1], axis_id, perm=by_rank))  45.3 us
    dot_general x1, matrix products, local(): jnp.einsum('jnk,pkw->pjnw', mixed, col_table, preferred_element_type=jnp....  12.7 us
    add x7, other arithmetic, joint_reduce(): first_pair[1] + second_pair[1]  8.2 us
    dot_general x1, matrix products, local(): jnp.einsum('pna,pjnb->pjab', sin_row, partial_g[..., width:], preferred_e...  7.18 us
    another operation x1, other arithmetic  6.2 us
    dot_general x1, matrix products, local(): jnp.einsum('pna,pjnb->pjab', cos_row, partial_g[..., :width], preferred_e...  5.84 us
    convert_element_type x1, other arithmetic, tables_for(): jnp.sin(angle).astype(jnp.bfloat16)  5.57 us
  transfers between devices with their start and end apart: 10, of which 8 were waited for; matrix products, arithmetic and copies ran while one was open for 6% of the time, Pallas kernels for 0%

profile of v1, /device:TPU:0, one launch (start us, length us, event | category | flops | bytes accessed | tf_op | source)
XLA Modules:
  0.0 221.2 jit_solution(1596857463300587191)
XLA Ops:
  7.2 3.2 %copy.14 = bf16[8,2,128,512]{3,2,0,1:T(8,128)(2,1)} copy(bf16[8,2,128,512]{3,2,1,0:T(8,128)(2,1)} %param.7) | data formatting | bytes 4194304 | tf_op args[1]
  10.5 3.0 %collective-permute-start = (bf16[1,2,64,512]{3,2,1,0:T(8,128)(2,1)S(1)}, bf16[1,2,64,512]{3,2,1,0:T(8,128)(2,1)S(1)}, u32[]{:S(2)}, u32[]{:S(2)}) collective-permute-start(bf16[1,2,64,512]{3,2,1,0:T(8,128)(2,1)S(1)} %copy-done.2), channel_id=1, source_target_pairs={{0,1},{1,2},{2,3},{3,4},{4,5},{5,6},{6,7},{7,0},{8,9},{9,10},{10,1... | collective-permute-start | bytes 393224 | tf_op jit(solution)/shard_map/ppermute | solution.py:24
  13.7 4.3 %fusion.37 = bf16[4,512,128]{1,2,0:T(8,128)(2,1)S(1)} fusion(s32[4,128]{1,0:T(4,128)S(1)} %get-tuple-element.160), kind=kLoop, calls=%fused_computation.59 | loop fusion | flops 4718592 | bytes 526336 | tf_op jit(solution)/shard_map/neg | solution.py:56
  17.9 5.6 %sine_convert_fusion.1 = (bf16[4,512,128]{1,2,0:T(8,128)(2,1)S(1)}, bf16[4,512,128]{1,2,0:T(8,128)(2,1)}) fusion(s32[4,128]{1,0:T(4,128)S(1)} %get-tuple-element.160), kind=kLoop, calls=%fused_computation.48 | loop fusion | flops 4194304 | bytes 1050624 | tf_op jit(solution)/shard_map/convert_element_type | solution.py:51
  23.7 1.6 collective-permute-start.1
  25.4 6.1 %collective-permute-done.1 = bf16[1,2,64,512]{3,2,1,0:T(8,128)(2,1)S(1)} collective-permute-done((bf16[1,2,64,512]{3,2,1,0:T(8,128)(2,1)S(1)}, bf16[1,2,64,512]{3,2,1,0:T(8,128)(2,1)S(1)}, u32[]{:S(2)}, u32[]{:S(2)}) %collective-permute-start.1) | collective-permute-done | bytes 131104 | tf_op jit(solution)/shard_map/ppermute | solution.py:24
  31.5 7.6 %collective-permute-done.2 = bf16[1,2,64,512]{3,2,1,0:T(8,128)(2,1)S(1)} collective-permute-done((bf16[1,2,64,512]{3,2,1,0:T(8,128)(2,1)S(1)}, bf16[1,2,64,512]{3,2,1,0:T(8,128)(2,1)S(1)}, u32[]{:S(2)}, u32[]{:S(2)}) %collective-permute-start.2) | collective-permute-done | bytes 131104 | tf_op jit(solution)/shard_map/ppermute | solution.py:24
  39.1 7.6 %collective-permute-done.3 = bf16[1,2,64,512]{3,2,1,0:T(8,128)(2,1)S(1)} collective-permute-done((bf16[1,2,64,512]{3,2,1,0:T(8,128)(2,1)S(1)}, bf16[1,2,64,512]{3,2,1,0:T(8,128)(2,1)S(1)}, u32[]{:S(2)}, u32[]{:S(2)}) %collective-permute-start.3) | collective-permute-done | bytes 131104 | tf_op jit(solution)/shard_map/ppermute | solution.py:24
  46.8 7.6 %collective-permute-done.4 = bf16[1,2,64,512]{3,2,1,0:T(8,128)(2,1)S(1)} collective-permute-done((bf16[1,2,64,512]{3,2,1,0:T(8,128)(2,1)S(1)}, bf16[1,2,64,512]{3,2,1,0:T(8,128)(2,1)S(1)}, u32[]{:S(2)}, u32[]{:S(2)}) %collective-permute-start.4) | collective-permute-done | bytes 131104 | tf_op jit(solution)/shard_map/ppermute | solution.py:24
  54.5 8.6 %collective-permute-done.5 = bf16[1,2,64,512]{3,2,1,0:T(8,128)(2,1)S(1)} collective-permute-done((bf16[1,2,64,512]{3,2,1,0:T(8,128)(2,1)S(1)}, bf16[1,2,64,512]{3,2,1,0:T(8,128)(2,1)S(1)}, u32[]{:S(2)}, u32[]{:S(2)}) %collective-permute-start.5) | collective-permute-done | bytes 131104 | tf_op jit(solution)/shard_map/ppermute | solution.py:24
  63.1 7.6 %collective-permute-done.6 = bf16[1,2,64,512]{3,2,1,0:T(8,128)(2,1)S(1)} collective-permute-done((bf16[1,2,64,512]{3,2,1,0:T(8,128)(2,1)S(1)}, bf16[1,2,64,512]{3,2,1,0:T(8,128)(2,1)S(1)}, u32[]{:S(2)}, u32[]{:S(2)}) %collective-permute-start.6) | collective-permute-done | bytes 131104 | tf_op jit(solution)/shard_map/ppermute | solution.py:24
  70.8 0.6 gather_fusion
  71.5 0.3 bitcast_convert_fusion
  71.9 6.2 %fusion.1 = (bf16[8,512,512]{2,1,0:T(8,128)(2,1)S(1)}, bf16[8,512,512]{2,1,0:T(8,128)(2,1)}) fusion(f32[512,512]{1,0:T(8,128)S(1)} %get-tuple-element.161, f32[512,512]{1,0:T(8,128)S(1)} %get-tuple-element.162, bf16[8,2,512,512]{3,2,0,1:T(8,128)(2,1)} %all-gather.6.cloned.1.call-done), kind=kLoop, calls=%fused_computation.8 | loop fusion | flops 20971520 | bytes 18874368 | tf_op jit(solution)/shard_map/convert.4
  78.1 12.7 %convert_bitcast_fusion = bf16[4,8,512,256]{2,3,1,0:T(8,128)(2,1)} fusion(bf16[8,512,512]{2,1,0:T(8,128)(2,1)} %get-tuple-element.152, bf16[8,512,512]{2,1,0:T(8,128)(2,1)S(1)} %get-tuple-element.151, bf16[4,512,128]{1,2,0:T(8,128)(2,1)S(1)} %copy-done.1, bf16[4,512,128]{1,2,0:T(8,128)(2,1)S(1)} %fusion.37, bf16[4,512,128]{1,2,0:T(8,128)(2,1)S(1)} %get-tuple-element.155), kind=kOutput, calls=%fused_computation.15 | convolution fusion | flops 8619294720 | bytes 18350080 | tf_op jit(solution)/shard_map/jnk,pkw->pjnw/dot_general | solution.py:86
  90.8 7.2 %fusion.7 = f32[4,8,128,128]{3,2,1,0:T(8,128)S(1)} fusion(bf16[4,8,512,256]{2,3,1,0:T(8,128)(2,1)} %convert_bitcast_fusion, s32[4,128]{1,0:T(4,128)S(1)} %get-tuple-element.159), kind=kOutput, calls=%fused_computation.16 | convolution fusion | flops 540803072 | bytes 6293504 | tf_op jit(solution)/shard_map/pna,pjnb->pjab/dot_general | solution.py:92
  98.0 5.8 %select_reduce_fusion = (f32[4,128,128]{2,1,0:T(8,128)S(1)}, f32[4,128,128]{2,1,0:T(8,128)S(1)}) fusion(pred[4,8]{1,0:T(4,128)(4,1)S(1)} %compare_reduce_fusion, f32[4,8,128,128]{3,2,1,0:T(8,128)S(1)} %fusion.7, s32[4,128]{1,0:T(4,128)S(1)} %get-tuple-element.159, bf16[4,8,512,256]{2,3,1,0:T(8,128)(2,1)S(1)} %copy-done.5), kind=kOutput, calls=%fused_computation.29 | convolution fusion | flops 544342016 | bytes 6818304 | tf_op jit(solution)/shard_map/pna,pjnb->pjab/dot_general | solution.py:89
  103.9 0.8 copy.17
  104.8 0.8 copy.18
  105.6 48.3 %all-gather.8.cloned.1.call-done = f32[32,128,128]{2,1,0:T(8,128)} async-done(((f32[4,128,128]{2,1,0:T(8,128)}), f32[32,128,128]{2,1,0:T(8,128)}) %all-gather.8.cloned.1.call-update) | async-done | bytes 2097168 | tf_op jit(solution)/shard_map/all_gather | solution.py:34
  154.0 1.0 slice.52
  154.9 49.5 %all-gather.10.cloned.1.call-done = f32[32,128,128]{2,1,0:T(8,128)} async-done(((f32[4,128,128]{2,1,0:T(8,128)}), f32[32,128,128]{2,1,0:T(8,128)}) %all-gather.10.cloned.1.call-update) | async-done | bytes 2097168 | tf_op jit(solution)/shard_map/all_gather | solution.py:34
  204.5 1.0 slice.53
  205.4 8.4 %while.17 = (s32[]{:T(128)}, f32[4,128,128]{2,1,0:T(8,128)S(1)}, f32[4,128,128]{2,1,0:T(8,128)S(1)}, f32[8,4,128,128]{3,2,1,0:T(8,128)}, f32[8,4,128,128]{3,2,1,0:T(8,128)}, /*index=5*/s32[]{:T(128)}, s32[]{:T(128)}, s32[]{:T(128)}) while((s32[]{:T(128)}, f32[4,128,128]{2,1,0:T(8,128)S(1)}, f32[4,128,128]{2,1,0:T(8,128)S(1)}, ...), condition=%wide.region_4.5_spmd, body=%wide.region_3.4_spmd.sunk | while | flops 131077 | bytes 1572995 | solution.py:40
  205.5 1.2 bitcast_add_fusion.2
  206.7 1.2 bitcast_add_fusion.2
  207.8 1.2 bitcast_add_fusion.2
  209.0 1.2 bitcast_add_fusion.2
  210.2 1.2 bitcast_add_fusion.2
  211.4 1.2 bitcast_add_fusion.2
  212.6 1.2 bitcast_add_fusion.2
  213.8 0.8 multiply_bitcast_fusion
  (41 shorter events, 0.7 us)
Async XLA Ops:
  7.2 3.3 %copy-start.2 = (bf16[1,2,64,512]{3,2,1,0:T(8,128)(2,1)S(1)}, bf16[1,2,64,512]{3,2,1,0:T(8,128)(2,1)}, u32[]{:S(2)}) copy-start(bf16[1,2,64,512]{3,2,1,0:T(8,128)(2,1)} %param.6) | copy-start | bytes 393220
  7.2 6.4 %copy-start.4 = (s32[1,4,2]{1,2,0:T(2,128)S(1)}, s32[1,4,2]{1,2,0:T(2,128)}, u32[]{:S(2)}) copy-start(s32[1,4,2]{1,2,0:T(2,128)} %param.8) | copy-start | bytes 100
  7.2 16.3 %copy-start.3 = (s32[1,4,48]{2,1,0:T(4,128)S(1)}, s32[1,4,48]{2,1,0:T(4,128)}, u32[]{:S(2)}) copy-start(s32[1,4,48]{2,1,0:T(4,128)} %param.9) | copy-start | bytes 2308
  7.2 64.7 %all-gather.6.cloned.1.call-start = ((), (), s32[]{:S(2)}) async-start(), calls=%async_computation | async-start | bytes 10485760 | tf_op jit(solution)/shard_map/all_gather | solution.py:85
  10.5 143.5 %all-gather.8.cloned.1.call-start = ((), (), s32[]{:S(2)}) async-start(), calls=%async_computation.1 | async-start | bytes 2359296 | tf_op jit(solution)/shard_map/all_gather | solution.py:34
  10.5 13.2 %collective-permute-start = (bf16[1,2,64,512]{3,2,1,0:T(8,128)(2,1)S(1)}, bf16[1,2,64,512]{3,2,1,0:T(8,128)(2,1)S(1)}, u32[]{:S(2)}, u32[]{:S(2)}) collective-permute-start(bf16[1,2,64,512]{3,2,1,0:T(8,128)(2,1)S(1)} %copy-done.2), channel_id=1, source_target_pairs={{0,1},{1,2},{2,3},{3,4},{4,5},{5,6},{6,7},{7,0},{8,9},{9,10},{10,1... | collective-permute-start | bytes 393224 | tf_op jit(solution)/shard_map/ppermute | solution.py:24
  23.7 7.7 %collective-permute-start.1 = (bf16[1,2,64,512]{3,2,1,0:T(8,128)(2,1)S(1)}, bf16[1,2,64,512]{3,2,1,0:T(8,128)(2,1)S(1)}, u32[]{:S(2)}, u32[]{:S(2)}) collective-permute-start(bf16[1,2,64,512]{3,2,1,0:T(8,128)(2,1)S(1)} %collective-permute-done), channel_id=1, source_target_pairs={{0,1},{1,2},{2,3},{3,4},{4,5},{5,6},{6,7},{7,0},{8,9},{9,10},{10,1... | collective-permute-start | bytes 393224 | tf_op jit(solution)/shard_map/ppermute | solution.py:24
  31.5 7.7 %collective-permute-start.2 = (bf16[1,2,64,512]{3,2,1,0:T(8,128)(2,1)S(1)}, bf16[1,2,64,512]{3,2,1,0:T(8,128)(2,1)S(1)}, u32[]{:S(2)}, u32[]{:S(2)}) collective-permute-start(bf16[1,2,64,512]{3,2,1,0:T(8,128)(2,1)S(1)} %collective-permute-done.1), channel_id=1, source_target_pairs={{0,1},{1,2},{2,3},{3,4},{4,5},{5,6},{6,7},{7,0},{8,9},{9,10},{10,1... | collective-permute-start | bytes 393224 | tf_op jit(solution)/shard_map/ppermute | solution.py:24
  39.1 7.7 %collective-permute-start.3 = (bf16[1,2,64,512]{3,2,1,0:T(8,128)(2,1)S(1)}, bf16[1,2,64,512]{3,2,1,0:T(8,128)(2,1)S(1)}, u32[]{:S(2)}, u32[]{:S(2)}) collective-permute-start(bf16[1,2,64,512]{3,2,1,0:T(8,128)(2,1)S(1)} %collective-permute-done.2), channel_id=1, source_target_pairs={{0,1},{1,2},{2,3},{3,4},{4,5},{5,6},{6,7},{7,0},{8,9},{9,10},{10,1... | collective-permute-start | bytes 393224 | tf_op jit(solution)/shard_map/ppermute | solution.py:24
  46.8 7.7 %collective-permute-start.4 = (bf16[1,2,64,512]{3,2,1,0:T(8,128)(2,1)S(1)}, bf16[1,2,64,512]{3,2,1,0:T(8,128)(2,1)S(1)}, u32[]{:S(2)}, u32[]{:S(2)}) collective-permute-start(bf16[1,2,64,512]{3,2,1,0:T(8,128)(2,1)S(1)} %collective-permute-done.3), channel_id=1, source_target_pairs={{0,1},{1,2},{2,3},{3,4},{4,5},{5,6},{6,7},{7,0},{8,9},{9,10},{10,1... | collective-permute-start | bytes 393224 | tf_op jit(solution)/shard_map/ppermute | solution.py:24
  54.5 8.6 %collective-permute-start.5 = (bf16[1,2,64,512]{3,2,1,0:T(8,128)(2,1)S(1)}, bf16[1,2,64,512]{3,2,1,0:T(8,128)(2,1)S(1)}, u32[]{:S(2)}, u32[]{:S(2)}) collective-permute-start(bf16[1,2,64,512]{3,2,1,0:T(8,128)(2,1)S(1)} %collective-permute-done.4), channel_id=1, source_target_pairs={{0,1},{1,2},{2,3},{3,4},{4,5},{5,6},{6,7},{7,0},{8,9},{9,10},{10,1... | collective-permute-start | bytes 393224 | tf_op jit(solution)/shard_map/ppermute | solution.py:24
  63.1 7.7 %collective-permute-start.6 = (bf16[1,2,64,512]{3,2,1,0:T(8,128)(2,1)S(1)}, bf16[1,2,64,512]{3,2,1,0:T(8,128)(2,1)S(1)}, u32[]{:S(2)}, u32[]{:S(2)}) collective-permute-start(bf16[1,2,64,512]{3,2,1,0:T(8,128)(2,1)S(1)} %collective-permute-done.5), channel_id=1, source_target_pairs={{0,1},{1,2},{2,3},{3,4},{4,5},{5,6},{6,7},{7,0},{8,9},{9,10},{10,1... | collective-permute-start | bytes 393224 | tf_op jit(solution)/shard_map/ppermute | solution.py:24
  71.9 6.2 %copy-start.1 = (bf16[4,512,128]{1,2,0:T(8,128)(2,1)S(1)}, bf16[4,512,128]{1,2,0:T(8,128)(2,1)}, u32[]{:S(2)}) copy-start(bf16[4,512,128]{1,2,0:T(8,128)(2,1)} %get-tuple-element.156) | copy-start | bytes 1572868
  90.8 7.2 %copy-start.5 = (bf16[4,8,512,256]{2,3,1,0:T(8,128)(2,1)S(1)}, bf16[4,8,512,256]{2,3,1,0:T(8,128)(2,1)}, u32[]{:S(2)}) copy-start(bf16[4,8,512,256]{2,3,1,0:T(8,128)(2,1)} %convert_bitcast_fusion) | copy-start | bytes 25165828
  104.7 99.7 %all-gather.10.cloned.1.call-start = ((), (), s32[]{:S(2)}) async-start(), calls=%async_computation.2 | async-start | bytes 2359296 | tf_op jit(solution)/shard_map/all_gather | solution.py:34
  213.8 0.8 copy-start
Sparse Core Ops, SparseCore 0:
  10.6 61.0 all-gather.5
  104.9 49.0 all-gather.7
  156.7 47.7 all-gather.9
